TPU v7x, 256 devices: a whole 4x4x8 slice. The times are simulated.
256 devices in a mesh: rep: 16 (over x, y_lo, core), blk: 16 (over y_hi, z).
Axes of the slice: x: 4, y: 4 (y_hi: 2, y_lo: 2; y = y_hi * 2 + y_lo), z: 8, core: 2. Of those that a mesh axis runs over, the one named last changes fastest.
Arguments:
- features: bfloat16 [65536, 1024], P(('rep', 'blk')), may hold values from -6 to 6
- weight: bfloat16 [1024, 1024], replicated, may hold values from -0.1875 to 0.1875
- bias: bfloat16 [1024], replicated, may hold values from -3 to 3
- tile_vals: bfloat16 [16, 16, 32, 4, 128, 128], P('rep', 'blk'), may hold values from -0.125 to 0.125
- tile_col: int32 [16, 16, 32, 4], P('rep', 'blk'), may hold values from 0 to 31
- tile_count: int32 [16, 16, 32], P('rep', 'blk'), may hold values from 0 to 4, as said below
Outputs:
- hidden: bfloat16 [65536, 1024], P(('rep', 'blk'))
Inputs may be any that keep to these rules, and one draw needn't show every extreme that they name: The first tile_count slots are the live ones; some entry equals 4 in every draw.
All inputs are finite; a program needn't handle non-finite values.
Results may differ from a plain program's by a relative error of at most 0.014.
Values may be sent and summed in bfloat16 or wider, within the bound.
No kernel may reach another device: no remote copies, remote signals or barrier semaphores. Data moves between devices by JAX's collectives and lax.ppermute only.
A program may use at most 64 MiB of HBM per device.

v0:
```python
import jax
import jax.numpy as jnp
from jax import lax
from jax.sharding import PartitionSpec as P


def term_maker(gathered, tile_block, col_index, live_count):
    tile_side = tile_block.shape[-1]
    slot_total = tile_block.shape[1]
    sources = gathered.reshape(-1, tile_side, gathered.shape[1])

    def block_sum(blk_id):
        block_tiles = tile_block[blk_id]
        block_cols = col_index[blk_id]
        block_live = live_count[blk_id]
        keep_mask = (jnp.arange(slot_total, dtype=jnp.int32) < block_live).astype(jnp.bfloat16)
        masked = block_tiles * keep_mask[:, None, None]
        picked = sources[block_cols]
        return jnp.einsum("kij,kjd->id", masked, picked, preferred_element_type=jnp.float32)

    def partial_term(start, count):
        block_ids = jnp.arange(count // tile_side, dtype=jnp.int32)
        return lax.map(block_sum, block_ids).reshape(count, -1)

    return partial_term


def body(features, weight, bias, tile_vals, tile_col, tile_count):
    tile_block = tile_vals[0, 0]
    col_index = tile_col[0, 0]
    live_count = tile_count[0, 0]
    row_total = features.shape[0]
    gathered = lax.all_gather(features, "rep", axis=0, tiled=True)
    summer = term_maker(gathered, tile_block, col_index, live_count)
    summed = lax.psum_scatter(
        summer(jnp.int32(0), row_total * lax.axis_size("blk")).astype(jnp.bfloat16),
        "blk",
        scatter_dimension=0,
        tiled=True,
    )
    mixed = jnp.dot(summed, weight, preferred_element_type=jnp.float32) + bias.astype(jnp.float32)
    return jnp.maximum(mixed, 0.0).astype(jnp.bfloat16)


def solution(mesh):
    return jax.shard_map(
        body,
        mesh=mesh,
        in_specs=(
            P(("rep", "blk"), None),
            P(),
            P(),
            P("rep", "blk", None, None, None, None),
            P("rep", "blk", None, None),
            P("rep", "blk", None),
        ),
        out_specs=P(("rep", "blk"), None),
        check_vma=False,
    )
```

profile of v0, /device:TPU:2, one launch (start us, length us, event | category | flops | bytes accessed | tf_op | source)
XLA Modules:
  0.0 625.8 jit_solution(16292536515272177173)
XLA Ops:
  8.1 58.6 %all-gather.2.cloned.1.call-done = bf16[4096,1024]{1,0:T(8,128)(2,1)} async-done(((bf16[256,1024]{1,0:T(8,128)(2,1)}), bf16[4096,1024]{1,0:T(8,128)(2,1)}) %all-gather.2.cloned.1.call-update) | async-done | bytes 8388624 | tf_op jit(solution)/shard_map/all_gather | solution.py:33
  66.7 322.8 %while.10 = (s32[]{:T(128)}, bf16[32,128,1024]{2,1,0:T(8,128)(2,1)}, s32[32]{0:T(128)S(1)}, bf16[32,4,128,128]{3,2,1,0:T(8,128)(2,1)}, s32[32]{0:T(128)}, /*inde...) while((s32[]{:T(128)}, bf16[32,128,1024]{2,1,0:T(8,128)(2,1)}, ...), condition=%wide.region_1.2_spmd, body=%wide.region_0.1_spmd.sunk | while | flops 134284320 | bytes 3805947 | solution.py:23
  69.0 4.0 gather_fusion
  74.8 2.0 fusion.16
  79.1 4.0 gather_fusion
  84.9 2.0 fusion.16
  89.2 4.0 gather_fusion
  95.0 2.0 fusion.16
  99.3 4.0 gather_fusion
  105.1 2.0 fusion.16
  109.4 4.0 gather_fusion
  119.4 4.0 gather_fusion
  125.3 2.0 fusion.16
  129.5 4.0 gather_fusion
  135.3 2.0 fusion.16
  139.6 4.0 gather_fusion
  145.4 2.0 fusion.16
  149.7 4.0 gather_fusion
  155.5 2.0 fusion.16
  159.8 4.0 gather_fusion
  165.6 2.0 fusion.16
  169.9 4.0 gather_fusion
  175.7 2.0 fusion.16
  179.9 4.0 gather_fusion
  185.8 2.0 fusion.16
  190.0 4.0 gather_fusion
  195.8 2.0 fusion.16
  200.1 4.0 gather_fusion
  205.9 2.0 fusion.16
  210.2 4.0 gather_fusion
  220.3 4.0 gather_fusion
  226.1 2.0 fusion.16
  230.3 4.0 gather_fusion
  236.2 2.0 fusion.16
  240.4 4.0 gather_fusion
  246.2 2.0 fusion.16
  250.5 4.0 gather_fusion
  256.4 2.0 fusion.16
  260.7 4.0 gather_fusion
  266.5 2.0 fusion.16
  270.7 4.0 gather_fusion
  276.6 2.0 fusion.16
  280.8 4.0 gather_fusion
  286.6 2.0 fusion.16
  290.9 4.0 gather_fusion
  301.0 4.0 gather_fusion
  311.0 4.0 gather_fusion
  316.9 2.0 fusion.16
  321.1 4.0 gather_fusion
  327.0 2.0 fusion.16
  331.2 4.0 gather_fusion
  337.0 2.0 fusion.16
  341.3 4.0 gather_fusion
  347.1 2.0 fusion.16
  351.4 4.0 gather_fusion
  357.2 2.0 fusion.16
  361.5 4.0 gather_fusion
  367.3 2.0 fusion.16
  371.6 4.0 gather_fusion
  377.4 2.0 fusion.16
  381.6 4.0 gather_fusion
  387.4 2.0 fusion.16
  390.1 226.2 %reduce-scatter.2.cloned.1.call-done = bf16[256,1024]{1,0:T(8,128)(2,1)} async-done(((bf16[4096,1024]{1,0:T(8,128)(2,1)}), bf16[256,1024]{1,0:T(8,128)(2,1)}) %reduce-scatter.2.cloned.1.call-update) | async-done | bytes 524304 | tf_op jit(solution)/shard_map/reduce_scatter | solution.py:35
  616.4 2.5 fusion.7
  (176 shorter events, 86.8 us)
Async XLA Ops:
  6.5 609.8 %copy-start = (bf16[1024,1024]{1,0:T(8,128)(2,1)S(1)}, bf16[1024,1024]{1,0:T(8,128)(2,1)}, u32[]{:S(2)}) copy-start(bf16[1024,1024]{1,0:T(8,128)(2,1)} %param.9) | copy-start | bytes 6291460
  6.5 60.1 %all-gather.2.cloned.1.call-start = ((), (), s32[]{:S(2)}) async-start(), calls=%async_computation.1 | async-start | bytes 8912896 | tf_op jit(solution)/shard_map/all_gather | solution.py:33
  7.3 609.1 %reduce-scatter.2.cloned.1.call-start = ((), (), s32[]{:S(2)}) async-start(), calls=%async_computation.2 | async-start | bytes 8912896 | tf_op jit(solution)/shard_map/reduce_scatter | solution.py:35
  389.4 0.7 copy-start.1
Sparse Core Ops, SparseCore 0:
  9.2 57.4 all-gather.1
  389.6 226.7 reduce-scatter.1
where the time goes:
time: 629 us; the launch traced here: 626 us
  waiting for transfers between devices  286 us (45%)
  local copies, waits for them, and re-layouts  187 us (30%)
  matrix products  65.6 us (10%)
  loops' own time  55.1 us (9%)
  other arithmetic  18.6 us (3%)
  between operations  13.4 us (2%)
    reduce_scatter x1, waiting for transfers between devices, body(): lax.psum_scatter(summer(jnp.int32(0), row_total * lax.axis_size('blk')).a...  226 us
    gather x32, local copies, waits for them, and re-layouts, block_sum(): picked = sources[block_cols]  128 us
    dot_general x32, matrix products, block_sum(): jnp.einsum('kij,kjd->id', masked, picked, preferred_element_type=jnp.floa...  63.1 us
    all_gather x1, waiting for transfers between devices, body(): gathered = lax.all_gather(features, 'rep', axis=0, tiled=True)  58.6 us
    another operation x1, loops' own time, partial_term(): return lax.map(block_sum, block_ids).reshape(count, -1)  55.1 us
    dynamic_slice x32, local copies, waits for them, and re-layouts, block_sum(): block_live = live_count[blk_id]  39.6 us
    dynamic_slice x32, local copies, waits for them, and re-layouts, partial_term(): return lax.map(block_sum, block_ids).reshape(count, -1)  18.5 us
    convert_element_type x32, other arithmetic, block_sum(): (jnp.arange(slot_total, dtype=jnp.int32) < block_live).astype(jnp.bfloat16)  18 us
  transfers between devices with their start and end apart: 2, of which 2 were waited for; matrix products, arithmetic and copies ran while one was open for 0% of the time, Pallas kernels for 0%

commit v1 on v0

--- a/solution.py
+++ b/solution.py
@@ -30,7 +30,10 @@
     col_index = tile_col[0, 0]
     live_count = tile_count[0, 0]
     row_total = features.shape[0]
-    gathered = lax.all_gather(features, "rep", axis=0, tiled=True)
+    gathered = jnp.concatenate(
+        lax.all_to_all(jnp.stack([features for _ in range(lax.psum(1, "rep"))]), "rep", 0, 0),
+        axis=0,
+    )
     summer = term_maker(gathered, tile_block, col_index, live_count)
     summed = lax.psum_scatter(
         summer(jnp.int32(0), row_total * lax.axis_size("blk")).astype(jnp.bfloat16),

time: 629 us -> 715 us (1.14)
  waiting for transfers between devices: 286 us -> 359 us
  loops' own time: 55.1 us -> 67.2 us
  local copies, waits for them, and re-layouts: 187 us -> 177 us
    all_to_all x0 -> x1, waiting for transfers between devices: none -> 99.4 us  [body(): lax.all_to_all(jnp.stack([features for _ in range(lax.psum(1, 'rep'))]),...]
    all_gather x1 -> x0, waiting for transfers between devices: 58.6 us -> none  [body(): gathered = lax.all_gather(features, 'rep', axis=0, tiled=True)]
    reduce_scatter x1, waiting for transfers between devices: 226 us -> 260 us  [body(): lax.psum_scatter(summer(jnp.int32(0), row_total * lax.axis_size('blk')).a...]
    dynamic_slice x32, local copies, waits for them, and re-layouts: 39.6 us -> 21.3 us  [block_sum(): block_live = live_count[blk_id]]
    another operation x1, loops' own time: 55.1 us -> 67.2 us  [partial_term(): return lax.map(block_sum, block_ids).reshape(count, -1)]
where the time goes in v1:
time: 715 us; the launch traced here: 711 us
  waiting for transfers between devices  359 us (50%)
  local copies, waits for them, and re-layouts  177 us (25%)
  loops' own time  67.2 us (9%)
  matrix products  65.5 us (9%)
  other arithmetic  22.6 us (3%)
  between operations  13.4 us (2%)
    reduce_scatter x1, waiting for transfers between devices, body(): lax.psum_scatter(summer(jnp.int32(0), row_total * lax.axis_size('blk')).a...  260 us
    gather x32, local copies, waits for them, and re-layouts, block_sum(): picked = sources[block_cols]  128 us
    all_to_all x1, waiting for transfers between devices, body(): lax.all_to_all(jnp.stack([features for _ in range(lax.psum(1, 'rep'))]),...  99.4 us
    another operation x1, loops' own time, partial_term(): return lax.map(block_sum, block_ids).reshape(count, -1)  67.2 us
    dot_general x32, matrix products, block_sum(): jnp.einsum('kij,kjd->id', masked, picked, preferred_element_type=jnp.floa...  63 us
    convert_element_type x32, other arithmetic, block_sum(): (jnp.arange(slot_total, dtype=jnp.int32) < block_live).astype(jnp.bfloat16)  22.1 us
    dynamic_slice x32, local copies, waits for them, and re-layouts, block_sum(): block_live = live_count[blk_id]  21.3 us
    dynamic_slice x32, local copies, waits for them, and re-layouts, partial_term(): return lax.map(block_sum, block_ids).reshape(count, -1)  21.1 us
  transfers between devices with their start and end apart: 2, of which 2 were waited for; matrix products, arithmetic and copies ran while one was open for 0% of the time, Pallas kernels for 0%

profile of v1, /device:TPU:2, one launch (start us, length us, event | category | flops | bytes accessed | tf_op | source)
XLA Modules:
  0.0 711.2 jit_solution(17492783388286250130)
XLA Ops:
  6.5 5.5 stack.2
  12.0 6.9 all-to-all-start
  19.1 99.4 %all-to-all-done = bf16[16,256,1024]{2,1,0:T(8,128)(2,1)} async-done(((bf16[16,256,1024]{2,1,0:T(8,128)(2,1)}), bf16[16,256,1024]{2,1,0:T(8,128)(2,1)}, u32[]{:S(2)}, u32[]{:S(2)}) %all-to-all-start) | async-done | bytes 8388640 | tf_op jit(solution)/shard_map/all_to_all | solution.py:34
  118.5 323.1 %while.10 = (s32[]{:T(128)}, bf16[32,128,1024]{2,1,0:T(8,128)(2,1)}, s32[32]{0:T(128)S(1)}, bf16[32,4,128,128]{3,2,1,0:T(8,128)(2,1)}, s32[32]{0:T(128)S(1)}, /*...) while((s32[]{:T(128)}, bf16[32,128,1024]{2,1,0:T(8,128)(2,1)}, ...), condition=%wide.region_1.2_spmd, body=%wide.region_0.1_spmd.sunk | while | flops 134284320 | bytes 3805947 | solution.py:23
  121.2 4.0 gather_fusion
  126.6 2.0 fusion.16
  131.4 4.0 gather_fusion
  136.7 2.0 fusion.16
  141.5 4.0 gather_fusion
  146.8 2.0 fusion.16
  151.6 4.0 gather_fusion
  156.9 2.0 fusion.16
  161.7 4.0 gather_fusion
  171.8 4.0 gather_fusion
  177.1 2.0 fusion.16
  181.9 4.0 gather_fusion
  187.2 2.0 fusion.16
  191.9 4.0 gather_fusion
  197.3 2.0 fusion.16
  202.0 4.0 gather_fusion
  207.4 2.0 fusion.16
  212.1 4.0 gather_fusion
  217.5 2.0 fusion.16
  222.2 4.0 gather_fusion
  227.6 2.0 fusion.16
  232.3 4.0 gather_fusion
  237.7 2.0 fusion.16
  242.4 4.0 gather_fusion
  247.8 2.0 fusion.16
  252.5 4.0 gather_fusion
  262.6 4.0 gather_fusion
  272.7 4.0 gather_fusion
  278.0 2.0 fusion.16
  282.8 4.0 gather_fusion
  288.1 2.0 fusion.16
  292.9 4.0 gather_fusion
  298.2 2.0 fusion.16
  303.0 4.0 gather_fusion
  308.4 2.0 fusion.16
  313.1 4.0 gather_fusion
  318.5 2.0 fusion.16
  323.2 4.0 gather_fusion
  328.6 2.0 fusion.16
  333.3 4.0 gather_fusion
  338.7 2.0 fusion.16
  343.4 4.0 gather_fusion
  353.5 4.0 gather_fusion
  363.5 4.0 gather_fusion
  368.9 2.0 fusion.16
  373.7 4.0 gather_fusion
  379.0 2.0 fusion.16
  383.7 4.0 gather_fusion
  389.1 2.0 fusion.16
  393.8 4.0 gather_fusion
  399.2 2.0 fusion.16
  403.9 4.0 gather_fusion
  409.3 2.0 fusion.16
  414.0 4.0 gather_fusion
  419.4 2.0 fusion.16
  424.1 4.0 gather_fusion
  434.2 4.0 gather_fusion
  439.6 2.0 fusion.16
  442.2 259.6 %reduce-scatter.2.cloned.1.call-done = bf16[256,1024]{1,0:T(8,128)(2,1)} async-done(((bf16[4096,1024]{1,0:T(8,128)(2,1)}), bf16[256,1024]{1,0:T(8,128)(2,1)}) %reduce-scatter.2.cloned.1.call-update) | async-done | bytes 524304 | tf_op jit(solution)/shard_map/reduce_scatter | solution.py:38
  701.8 2.5 fusion.7
  (180 shorter events, 77.5 us)
Async XLA Ops:
  6.5 695.3 %copy-start = (bf16[1024,1024]{1,0:T(8,128)(2,1)S(1)}, bf16[1024,1024]{1,0:T(8,128)(2,1)}, u32[]{:S(2)}) copy-start(bf16[1024,1024]{1,0:T(8,128)(2,1)} %param.9) | copy-start | bytes 6291460
  12.0 6.9 copy-start.1
  12.0 106.4 %copy-start.3 = (s32[1,1,32]{2,1,0:T(1,128)S(1)}, s32[1,1,32]{2,1,0:T(1,128)}, u32[]{:S(2)}) copy-start(s32[1,1,32]{2,1,0:T(1,128)} %param.13) | copy-start | bytes 388
  12.0 106.4 %all-to-all-start = ((bf16[16,256,1024]{2,1,0:T(8,128)(2,1)}), bf16[16,256,1024]{2,1,0:T(8,128)(2,1)}, u32[]{:S(2)}, u32[]{:S(2)}) async-start(bf16[16,256,1024]{2,1,0:T(8,128)(2,1)} %stack.2), calls=%async_computation | async-start | bytes 16777216 | tf_op jit(solution)/shard_map/all_to_all | solution.py:34
  18.9 682.9 %reduce-scatter.2.cloned.1.call-start = ((), (), s32[]{:S(2)}) async-start(), calls=%async_computation.2 | async-start | bytes 8912896 | tf_op jit(solution)/shard_map/reduce_scatter | solution.py:38
  441.5 0.7 copy-start.2
Sparse Core Ops, SparseCore 0:
  441.7 260.1 reduce-scatter.1
